TPU v7x, 512 devices: a whole 4x4x16 slice. The times are simulated.
512 devices in a mesh: ctx: 32 (over z_hi, x, y), exp: 16 (over z_lo, core).
Axes of the slice: x: 4, y: 4, z: 16 (z_hi: 2, z_lo: 8; z = z_hi * 8 + z_lo), core: 2. Of those that a mesh axis runs over, the one named last changes fastest.
Arguments:
- residual: bfloat16 [4096, 4096], P(('ctx', 'exp')), may hold values from -6 to 6
- queries: bfloat16 [4096, 4096], P('ctx', 'exp'), may hold values from -8 to 8
- keys: bfloat16 [4096, 256], P('ctx'), may hold values from -8 to 8
- values: bfloat16 [4096, 256], P('ctx'), may hold values from -6 to 6
- span_pos: int32 [64], replicated, may hold values from 0 to 63, each once
- out_proj: bfloat16 [4096, 4096], P('exp'), may hold values from -0.71875 to 0.71875
- norm_gain: float32 [4096], replicated, may hold values from 0.25 to 1.75
- expert_gate: bfloat16 [16, 4096, 768], P('exp', None, 'ctx'), may hold values from -0.09375 to 0.09375
- expert_up: bfloat16 [16, 4096, 768], P('exp', None, 'ctx'), may hold values from -0.09375 to 0.09375
- expert_ids: int32 [4096, 8], P(('ctx', 'exp')), may hold values from 0 to 15, all different within a row; in each aligned block of 8 rows (0 to 7, 8 to 15, ...) at most 6 rows name the same one
- route_weight: float32 [4096, 8], P(('ctx', 'exp')), may hold values from 0.25 to 2
Outputs:
- mixed: bfloat16 [4096, 4096], P(('ctx', 'exp'))
- routed: bfloat16 [4096, 8, 768], P(('ctx', 'exp'))
Inputs may be any that keep to these rules, and one draw needn't show every extreme that they name: `span_pos`: every span number appears once. `expert_ids`: each row names 8 different experts; among the rows of one device (8 rows in a row, aligned) no expert is named more than 6 times, and in some device's rows some expert is named exactly 6 times.
All inputs are finite; a program needn't handle non-finite values.
Results may differ from a plain program's by a relative error of at most 0.035.
Values may be sent and summed in bfloat16 or wider, within the bound.
No kernel may reach another device: no remote copies, remote signals or barrier semaphores. Data moves between devices by JAX's collectives and lax.ppermute only.
A program may use at most 128 MiB of HBM per device.

v0:
```python
import math
import jax
import jax.numpy as jnp
import numpy as np
from jax import lax
from jax.sharding import Mesh
from jax.sharding import PartitionSpec as P

D = 4096
HQ = 32
KVH = 2
HD = 128
FE = 768
EXPERTS = 16
TOPK = 8
CH = 64
CTX = ("zh", "x", "y")
EXP = ("zl", "c")


def stored_positions(span_pos, rows):
    span = rows // CH
    table = span[:, None] == jnp.arange(span_pos.shape[0], dtype=jnp.int32)[None, :]
    base = jnp.sum(jnp.where(table, span_pos[None, :], 0), axis=1)
    return base * CH + rows % CH


def doubling_bits(n):
    bits = []
    b = n // 2
    while b >= 1:
        bits.append(b)
        b //= 2
    return bits


def gather_by_doubling(piece, n):
    idx = lax.axis_index(CTX)
    cur = piece
    order = [0]
    for bit in doubling_bits(n):
        other = lax.ppermute(cur, CTX, [(i, i ^ bit) for i in range(n)])
        low = idx & bit == 0
        cur = jnp.where(low, jnp.concatenate([cur, other]), jnp.concatenate([other, cur]))
        order = order + [o + bit for o in order]
    return (cur, order)


def shards(
    residual,
    queries,
    keys,
    values,
    span_pos,
    out_proj,
    norm_gain,
    expert_gate,
    expert_up,
    expert_ids,
    route_weight,
    n_ctx,
    n_xy,
    n_zh,
):
    tok_rows = queries.shape[0]
    per_device = queries.shape[1] // HD
    group = HQ // KVH
    ctx_index = lax.axis_index(CTX)
    exp_index = lax.axis_index(EXP)
    n_exp = EXPERTS
    fe_dev = expert_gate.shape[2]
    w_local = jnp.concatenate([expert_gate[0].T, expert_up[0].T], axis=0)
    w_all = lax.all_gather(w_local, "zh", axis=0, tiled=True)
    w_all = lax.all_gather(w_all, ("x", "y"), axis=0, tiled=True)
    kv_head = exp_index * per_device // group
    own_keys = lax.dynamic_slice_in_dim(keys, kv_head * HD, HD, 1)
    own_values = lax.dynamic_slice_in_dim(values, kv_head * HD, HD, 1)
    kv_local = jnp.concatenate([own_keys, own_values], axis=1)
    kv_all, order = gather_by_doubling(kv_local, n_ctx)
    key_piece = kv_all[:, :HD]
    value_piece = kv_all[:, HD:]
    length = key_piece.shape[0]
    block_ctx = jnp.asarray(np.array(order, np.int32))
    key_rows_all = jnp.repeat(block_ctx, tok_rows) * tok_rows + jnp.tile(
        jnp.arange(tok_rows, dtype=jnp.int32), n_ctx
    )
    query_pos = stored_positions(
        span_pos, ctx_index * tok_rows + jnp.arange(tok_rows, dtype=jnp.int32)
    )
    query_heads = queries.reshape(tok_rows, per_device, HD)
    scale = 1.0 / math.sqrt(HD)
    carry = (
        jnp.full((per_device, tok_rows), -1e30, jnp.float32),
        jnp.zeros((per_device, tok_rows), jnp.float32),
        jnp.zeros((per_device, tok_rows, HD), jnp.float32),
    )
    block = min(length, 1024)
    for begin in range(0, length, block):
        stop = min(begin + block, length)
        attend_key_piece = key_piece[begin:stop]
        attend_value_piece = value_piece[begin:stop]
        attend_running, attend_total, attend_accum = carry
        key_pos = stored_positions(span_pos, key_rows_all[begin:stop])
        scores = (
            jnp.einsum(
                "tqd,nd->qtn", query_heads, attend_key_piece, preferred_element_type=jnp.float32
            )
            * scale
        )
        visible = key_pos[None, None, :] <= query_pos[None, :, None]
        block_top = jnp.max(jnp.where(visible, scores, -1e30), axis=2)
        new_top = jnp.maximum(attend_running, block_top)
        factor = jnp.exp(attend_running - new_top)
        probs = jnp.where(visible, jnp.exp(scores - new_top[:, :, None]), 0.0)
        attend_total = attend_total * factor + jnp.sum(probs, axis=2)
        summed = jnp.einsum(
            "qtn,nd->qtd",
            probs.astype(jnp.bfloat16),
            attend_value_piece,
            preferred_element_type=jnp.float32,
        )
        attend_accum = attend_accum * factor[:, :, None] + summed
        carry = (new_top, attend_total, attend_accum)
    running, total, accum = carry
    attn = (accum / total[:, :, None]).astype(jnp.bfloat16)
    attn = jnp.transpose(attn, (1, 0, 2)).reshape(tok_rows, per_device * HD)
    tok_dev = residual.shape[0]
    share = jnp.dot(attn, out_proj, preferred_element_type=jnp.float32).astype(jnp.bfloat16)
    shares = lax.all_to_all(
        share.reshape(n_exp, tok_dev, D), EXP, split_axis=0, concat_axis=0, tiled=True
    )
    head_total = jnp.sum(shares.astype(jnp.float32), axis=0)
    mixed = (residual.astype(jnp.float32) + head_total).astype(jnp.bfloat16)
    mixed_f = mixed.astype(jnp.float32)
    square = jnp.mean(mixed_f * mixed_f, axis=1, keepdims=True)
    normed = (mixed_f * lax.rsqrt(square + 1e-06) * norm_gain[None, :]).astype(jnp.bfloat16)
    most_slots = 3 * tok_dev // 4
    ids_flat = expert_ids.reshape(-1)
    onehot = (ids_flat[:, None] == jnp.arange(EXPERTS, dtype=jnp.int32)[None, :]).astype(jnp.int32)
    earlier = jnp.cumsum(onehot, axis=0) - onehot
    slot = jnp.sum(earlier * onehot, axis=1)
    target = ids_flat * most_slots + slot
    placing = (
        target[:, None] == jnp.arange(EXPERTS * most_slots, dtype=jnp.int32)[None, :]
    ).astype(jnp.bfloat16)
    placing = jnp.sum(placing.reshape(tok_dev, TOPK, EXPERTS * most_slots), axis=1)
    outgoing = jnp.einsum("ts,td->sd", placing, normed, preferred_element_type=jnp.float32).astype(
        jnp.bfloat16
    )
    outgoing = outgoing.reshape(EXPERTS, most_slots, D)
    received = lax.all_to_all(outgoing, EXP, split_axis=0, concat_axis=0, tiled=True)
    received = received.reshape(EXPERTS * most_slots, D)
    proj = jnp.einsum("sd,fd->sf", received, w_all, preferred_element_type=jnp.float32)
    proj = proj.reshape(EXPERTS * most_slots, n_xy, n_zh, 2, fe_dev)
    hidden = jax.nn.silu(proj[:, :, :, 0]) * proj[:, :, :, 1]
    hidden = jnp.transpose(hidden, (0, 2, 1, 3)).reshape(EXPERTS, most_slots, FE)
    returned = (
        lax.all_to_all(hidden.astype(jnp.bfloat16), EXP, split_axis=0, concat_axis=0, tiled=True)
        .astype(jnp.float32)
        .reshape(EXPERTS * most_slots, FE)
    )
    picked = jnp.take(returned, target, axis=0)
    routed = (picked * route_weight.reshape(-1)[:, None]).astype(jnp.bfloat16)
    return (mixed, routed.reshape(tok_dev, TOPK, FE))


def solution(mesh):
    n_ctx = mesh.shape["ctx"]
    n_exp = mesh.shape["exp"]
    n_zh = 2
    n_xy = n_ctx // n_zh
    side = int(round(math.sqrt(n_xy)))
    n_zl = n_exp // 2
    fine = Mesh(mesh.devices.reshape(n_zh, side, n_xy // side, n_zl, 2), CTX + EXP)
    tok = CTX + EXP
    in_specs = (
        P(tok, None),
        P(CTX, EXP),
        P(CTX, None),
        P(CTX, None),
        P(),
        P(EXP, None),
        P(),
        P(EXP, None, CTX),
        P(EXP, None, CTX),
        P(tok, None),
        P(tok, None),
    )
    out_specs = (P(tok, None), P(tok, None, None))

    def body(*args):
        return shards(*args, n_ctx=n_ctx, n_xy=n_xy, n_zh=n_zh)

    return jax.shard_map(body, mesh=fine, in_specs=in_specs, out_specs=out_specs, check_vma=False)
```

profile of v0, /device:TPU:269, one launch (start us, length us, event | category | flops | bytes accessed | tf_op | source)
XLA Modules:
  0.0 315.9 jit_solution(2825617987332319186)
XLA Ops:
  7.2 1.2 pad_maximum_fusion
  8.5 23.8 %all_gather.6 = bf16[96,4096]{1,0:T(8,128)(2,1)} all-gather(bf16[48,4096]{1,0:T(8,128)(2,1)S(1)} %pad_maximum_fusion), channel_id=1, replica_groups=mesh['zh'=2,'x'=4,'y'=4,'zl'=8,'c'=2] {'zh'}, dimensions={0}, use_global_device_ids=true | all-gather | bytes 1179648 | tf_op jit(solution)/shard_map/all_gather | solution.py:73
  32.4 2.1 collective-permute-start
  34.5 19.4 %collective-permute-done = bf16[128,256]{1,0:T(8,128)(2,1)S(1)} collective-permute-done((bf16[128,256]{1,0:T(8,128)(2,1)S(1)}, bf16[128,256]{1,0:T(8,128)(2,1)S(1)}, u32[]{:S(2)}, u32[]{:S(2)}) %collective-permute-start) | collective-permute-done | bytes 65568 | tf_op jit(solution)/shard_map/ppermute | solution.py:42
  54.0 2.1 collective-permute-start.1
  56.1 5.6 %collective-permute-done.1 = bf16[256,256]{1,0:T(8,128)(2,1)S(1)} collective-permute-done((bf16[256,256]{1,0:T(8,128)(2,1)S(1)}, bf16[256,256]{1,0:T(8,128)(2,1)S(1)}, u32[]{:S(2)}, u32[]{:S(2)}) %collective-permute-start.1) | collective-permute-done | bytes 131104 | tf_op jit(solution)/shard_map/ppermute | solution.py:42
  61.9 2.8 collective-permute-start.2
  64.7 5.3 %collective-permute-done.2 = bf16[512,256]{1,0:T(8,128)(2,1)S(1)} collective-permute-done((bf16[512,256]{1,0:T(8,128)(2,1)S(1)}, bf16[512,256]{1,0:T(8,128)(2,1)S(1)}, u32[]{:S(2)}, u32[]{:S(2)}) %collective-permute-start.2) | collective-permute-done | bytes 262176 | tf_op jit(solution)/shard_map/ppermute | solution.py:42
  70.3 3.9 %collective-permute-start.3 = (bf16[1024,256]{1,0:T(8,128)(2,1)S(1)}, bf16[1024,256]{1,0:T(8,128)(2,1)S(1)}, u32[]{:S(2)}, u32[]{:S(2)}) collective-permute-start(bf16[1024,256]{1,0:T(8,128)(2,1)S(1)} %maximum_select_fusion.2), channel_id=1, source_target_pairs={{0,32},{16,48},{32,0},{48,16},{64,96},{80,112},{96,64},{112,80},{1... | collective-permute-start | bytes 1572872 | tf_op jit(solution)/shard_map/ppermute | solution.py:42
  74.4 21.2 %collective-permute-done.3 = bf16[1024,256]{1,0:T(8,128)(2,1)S(1)} collective-permute-done((bf16[1024,256]{1,0:T(8,128)(2,1)S(1)}, bf16[1024,256]{1,0:T(8,128)(2,1)S(1)}, u32[]{:S(2)}, u32[]{:S(2)}) %collective-permute-start.3) | collective-permute-done | bytes 524320 | tf_op jit(solution)/shard_map/ppermute | solution.py:42
  95.8 3.1 collective-permute-start.4
  99.3 0.8 broadcast_compare_fusion.1
  100.1 19.2 %collective-permute-done.4 = bf16[2048,256]{1,0:T(8,128)(2,1)S(1)} collective-permute-done((bf16[2048,256]{1,0:T(8,128)(2,1)S(1)}, bf16[2048,256]{1,0:T(8,128)(2,1)S(1)}, u32[]{:S(2)}, u32[]{:S(2)}) %collective-permute-start.4) | collective-permute-done | bytes 1048608 | tf_op jit(solution)/shard_map/ppermute | solution.py:42
  119.3 0.5 maximum_select_fusion
  121.2 0.4 fusion.14
  121.7 0.4 fusion.18
  122.1 0.4 fusion.12
  122.5 0.4 fusion.10
  123.6 1.5 fusion
  125.1 42.7 %all-to-all-start = ((bf16[16,8,4096]{2,1,0:T(8,128)(2,1)}), bf16[16,8,4096]{2,1,0:T(8,128)(2,1)S(1)}, u32[]{:S(2)}, u32[]{:S(2)}) async-start(bf16[16,8,4096]{2,1,0:T(8,128)(2,1)} %fusion), calls=%async_computation | async-start | bytes 2097152 | tf_op jit(solution)/shard_map/all_to_all | solution.py:129
  168.5 43.8 %all-to-all-done = bf16[16,8,4096]{2,1,0:T(8,128)(2,1)S(1)} async-done(((bf16[16,8,4096]{2,1,0:T(8,128)(2,1)}), bf16[16,8,4096]{2,1,0:T(8,128)(2,1)S(1)}, u32[]{:S(2)}, u32[]{:S(2)}) %all-to-all-start) | async-done | bytes 1048608 | tf_op jit(solution)/shard_map/all_to_all | solution.py:129
  212.6 1.3 convolution_convert_fusion.1
  213.9 1.4 reshape.361
  215.3 60.6 %all_to_all.15 = bf16[16,6,4096]{2,1,0:T(8,128)(2,1)} all-to-all(bf16[16,6,4096]{2,1,0:T(8,128)(2,1)S(1)} %reshape.361), channel_id=1, replica_groups=mesh['zh'=2,'x'=4,'y'=4,'zl'=8,'c'=2] {'zl','c'}, dimensions={0} | all-to-all | bytes 1572864 | tf_op jit(solution)/shard_map/all_to_all | solution.py:151
  276.0 1.4 reshape.383
  277.4 6.4 %fusion.22 = f32[96,16,2,2,24]{0,4,3,2,1:T(8,128)S(1)} fusion(bf16[16,2,2,24,4096]{4,3,2,1,0:T(8,128)(2,1)} %bitcast.294, bf16[96,4096,1,1,1]{1,0,2,3,4:T(8,128)(2,1)S(1)} %reshape.383), kind=kOutput, calls=%fused_computation.44 | convolution fusion | flops 1207959552 | bytes 13959168 | tf_op jit(solution)/shard_map/sd,fd->sf/dot_general | solution.py:153
  284.0 1.1 copy.54
  285.1 1.8 convert_element_type.76
  286.9 6.1 %all-to-all-start.2 = ((bf16[16,6,768]{2,1,0:T(8,128)(2,1)}), bf16[16,6,768]{2,1,0:T(8,128)(2,1)S(1)}, u32[]{:S(2)}, u32[]{:S(2)}) async-start(bf16[16,6,768]{2,1,0:T(8,128)(2,1)} %convert_element_type.76), calls=%async_computation.2 | async-start | bytes 393216 | tf_op jit(solution)/shard_map/all_to_all | solution.py:158
  293.0 14.6 %all-to-all-done.2 = bf16[16,6,768]{2,1,0:T(8,128)(2,1)S(1)} async-done(((bf16[16,6,768]{2,1,0:T(8,128)(2,1)}), bf16[16,6,768]{2,1,0:T(8,128)(2,1)S(1)}, u32[]{:S(2)}, u32[]{:S(2)}) %all-to-all-start.2) | async-done | bytes 147488 | tf_op jit(solution)/shard_map/all_to_all | solution.py:158
  307.7 0.7 gather_fusion
  308.4 0.7 fusion.43
  (63 shorter events, 4.5 us)
Async XLA Ops:
  7.2 116.4 %copy-start = (bf16[256,4096]{1,0:T(8,128)(2,1)S(1)}, bf16[256,4096]{1,0:T(8,128)(2,1)}, u32[]{:S(2)}) copy-start(bf16[256,4096]{1,0:T(8,128)(2,1)} %param.17) | copy-start | bytes 6291460
  7.2 25.2 %copy-start.5 = (bf16[128,256]{1,0:T(8,128)(2,1)S(1)}, bf16[128,256]{1,0:T(8,128)(2,1)}, u32[]{:S(2)}) copy-start(bf16[128,256]{1,0:T(8,128)(2,1)} %param.15) | copy-start | bytes 196612
  7.2 25.2 %copy-start.6 = (bf16[128,256]{1,0:T(8,128)(2,1)S(1)}, bf16[128,256]{1,0:T(8,128)(2,1)}, u32[]{:S(2)}) copy-start(bf16[128,256]{1,0:T(8,128)(2,1)} %param.14) | copy-start | bytes 196612
  7.2 270.2 %all-gather.2.cloned.1.call-start = ((), (), s32[]{:S(2)}) async-start(), calls=%async_computation.3 | async-start | bytes 13369344 | tf_op jit(solution)/shard_map/all_gather | solution.py:74
  8.4 65.8 %copy-start.8 = (s32[64]{0:T(128)S(1)}, s32[64]{0:T(128)}, u32[]{:S(2)}) copy-start(s32[64]{0:T(128)} %param.16) | copy-start | bytes 772
  8.5 65.9 %copy-start.9 = (s32[32]{0:T(128)S(1)}, s32[32]{0:T(128)}, u32[]{:S(2)}) copy-start(s32[32]{0:T(128)} %constant.180) | copy-start | bytes 388
  32.4 21.5 %collective-permute-start = (bf16[128,256]{1,0:T(8,128)(2,1)S(1)}, bf16[128,256]{1,0:T(8,128)(2,1)S(1)}, u32[]{:S(2)}, u32[]{:S(2)}) collective-permute-start(bf16[128,256]{1,0:T(8,128)(2,1)S(1)} %pad_maximum_fusion.1), channel_id=1, source_target_pairs={{0,256},{16,272},{32,288},{48,304},{64,320},{80,336},{96,352},{112... | collective-permute-start | bytes 196616 | tf_op jit(solution)/shard_map/ppermute | solution.py:42
  54.0 7.8 %collective-permute-start.1 = (bf16[256,256]{1,0:T(8,128)(2,1)S(1)}, bf16[256,256]{1,0:T(8,128)(2,1)S(1)}, u32[]{:S(2)}, u32[]{:S(2)}) collective-permute-start(bf16[256,256]{1,0:T(8,128)(2,1)S(1)} %maximum_select_fusion.4), channel_id=1, source_target_pairs={{0,128},{16,144},{32,160},{48,176},{64,192},{80,208},{96,224},{112... | collective-permute-start | bytes 393224 | tf_op jit(solution)/shard_map/ppermute | solution.py:42
  61.9 8.2 %collective-permute-start.2 = (bf16[512,256]{1,0:T(8,128)(2,1)S(1)}, bf16[512,256]{1,0:T(8,128)(2,1)S(1)}, u32[]{:S(2)}, u32[]{:S(2)}) collective-permute-start(bf16[512,256]{1,0:T(8,128)(2,1)S(1)} %maximum_select_fusion.3), channel_id=1, source_target_pairs={{0,64},{16,80},{32,96},{48,112},{64,0},{80,16},{96,32},{112,48},{1... | collective-permute-start | bytes 786440 | tf_op jit(solution)/shard_map/ppermute | solution.py:42
  70.3 25.3 %collective-permute-start.3 = (bf16[1024,256]{1,0:T(8,128)(2,1)S(1)}, bf16[1024,256]{1,0:T(8,128)(2,1)S(1)}, u32[]{:S(2)}, u32[]{:S(2)}) collective-permute-start(bf16[1024,256]{1,0:T(8,128)(2,1)S(1)} %maximum_select_fusion.2), channel_id=1, source_target_pairs={{0,32},{16,48},{32,0},{48,16},{64,96},{80,112},{96,64},{112,80},{1... | collective-permute-start | bytes 1572872 | tf_op jit(solution)/shard_map/ppermute | solution.py:42
  95.8 23.5 %collective-permute-start.4 = (bf16[2048,256]{1,0:T(8,128)(2,1)S(1)}, bf16[2048,256]{1,0:T(8,128)(2,1)S(1)}, u32[]{:S(2)}, u32[]{:S(2)}) collective-permute-start(bf16[2048,256]{1,0:T(8,128)(2,1)S(1)} %maximum_select_fusion.1), channel_id=1, source_target_pairs={{0,16},{16,0},{32,48},{48,32},{64,80},{80,64},{96,112},{112,96},{1... | collective-permute-start | bytes 3145736 | tf_op jit(solution)/shard_map/ppermute | solution.py:42
  100.1 19.8 %copy-start.10 = (bf16[128,256]{1,0:T(8,128)(2,1)S(1)}, bf16[128,256]{1,0:T(8,128)(2,1)}, u32[]{:S(2)}) copy-start(bf16[128,256]{1,0:T(8,128)(2,1)} %param.13) | copy-start | bytes 196612
  123.6 44.3 %copy-start.3 = (s32[8,8]{1,0:T(8,128)S(1)}, s32[8,8]{1,0:T(8,128)}, u32[]{:S(2)}) copy-start(s32[8,8]{1,0:T(8,128)} %param.21) | copy-start | bytes 772
  125.1 87.3 %copy-start.2 = (bf16[8,4096]{1,0:T(8,128)(2,1)S(1)}, bf16[8,4096]{1,0:T(8,128)(2,1)}, u32[]{:S(2)}) copy-start(bf16[8,4096]{1,0:T(8,128)(2,1)} %param.12) | copy-start | bytes 196612
  125.1 87.5 %copy-start.4 = (f32[4096]{0:T(1024)S(1)}, f32[4096]{0:T(1024)}, u32[]{:S(2)}) copy-start(f32[4096]{0:T(1024)} %param.18) | copy-start | bytes 49156
  125.1 87.1 %all-to-all-start = ((bf16[16,8,4096]{2,1,0:T(8,128)(2,1)}), bf16[16,8,4096]{2,1,0:T(8,128)(2,1)S(1)}, u32[]{:S(2)}, u32[]{:S(2)}) async-start(bf16[16,8,4096]{2,1,0:T(8,128)(2,1)} %fusion), calls=%async_computation | async-start | bytes 2097152 | tf_op jit(solution)/shard_map/all_to_all | solution.py:129
  212.6 63.4 %copy-start.1 = (bf16[8,4096]{1,0:T(8,128)(2,1)}, bf16[8,4096]{1,0:T(8,128)(2,1)S(1)}, u32[]{:S(2)}) copy-start(bf16[8,4096]{1,0:T(8,128)(2,1)S(1)} %get-tuple-element.9) | copy-start | bytes 196612
  284.0 24.4 %copy-start.7 = (f32[8,8]{1,0:T(8,128)S(1)}, f32[8,8]{1,0:T(8,128)}, u32[]{:S(2)}) copy-start(f32[8,8]{1,0:T(8,128)} %param.22) | copy-start | bytes 772
  286.9 20.7 %all-to-all-start.2 = ((bf16[16,6,768]{2,1,0:T(8,128)(2,1)}), bf16[16,6,768]{2,1,0:T(8,128)(2,1)S(1)}, u32[]{:S(2)}, u32[]{:S(2)}) async-start(bf16[16,6,768]{2,1,0:T(8,128)(2,1)} %convert_element_type.76), calls=%async_computation.2 | async-start | bytes 393216 | tf_op jit(solution)/shard_map/all_to_all | solution.py:158
Sparse Core Ops, SparseCore 0:
  32.4 141.4 all-gather.1
where the time goes:
time: 316 us
  waiting for transfers between devices  129 us (41%)
  blocking collectives  84.5 us (27%)
  starting transfers between devices  62.9 us (20%)
  between operations  14.5 us (5%)
  matrix products  12.1 us (4%)
  local copies, waits for them, and re-layouts  6.76 us (2%)
  other arithmetic  6.11 us (2%)
    ppermute x5, waiting for transfers between devices, gather_by_doubling(): other = lax.ppermute(cur, CTX, [(i, i ^ bit) for i in range(n)])  70.8 us
    all_to_all x1, blocking collectives, shards(): lax.all_to_all(outgoing, EXP, split_axis=0, concat_axis=0, tiled=True)  60.6 us
    all_to_all x1, waiting for transfers between devices, shards(): lax.all_to_all(share.reshape(n_exp, tok_dev, D), EXP, split_axis=0, conca...  43.8 us
    all_to_all x1, starting transfers between devices, shards(): lax.all_to_all(share.reshape(n_exp, tok_dev, D), EXP, split_axis=0, conca...  42.7 us
    all_gather x1, blocking collectives, shards(): w_all = lax.all_gather(w_local, 'zh', axis=0, tiled=True)  23.8 us
    all_to_all x1, waiting for transfers between devices, shards(): lax.all_to_all(hidden.astype(jnp.bfloat16), EXP, split_axis=0, concat_axi...  14.6 us
    ppermute x5, starting transfers between devices, gather_by_doubling(): other = lax.ppermute(cur, CTX, [(i, i ^ bit) for i in range(n)])  14.1 us
    dot_general x1, matrix products, shards(): jnp.einsum('sd,fd->sf', received, w_all, preferred_element_type=jnp.float32)  6.41 us
  transfers between devices with their start and end apart: 8, of which 7 were waited for; matrix products, arithmetic and copies ran while one was open for 4% of the time, Pallas kernels for 0%

commit v1 on v0

--- a/solution.py
+++ b/solution.py
@@ -70,7 +70,9 @@
     n_exp = EXPERTS
     fe_dev = expert_gate.shape[2]
     w_local = jnp.concatenate([expert_gate[0].T, expert_up[0].T], axis=0)
-    w_all = lax.all_gather(w_local, "zh", axis=0, tiled=True)
+    w_all = jnp.concatenate(
+        lax.all_to_all(jnp.stack([w_local] * lax.axis_size("zh")), "zh", 0, 0), axis=0
+    )
     w_all = lax.all_gather(w_all, ("x", "y"), axis=0, tiled=True)
     kv_head = exp_index * per_device // group
     own_keys = lax.dynamic_slice_in_dim(keys, kv_head * HD, HD, 1)

time: 316 us -> 330 us (1.044)
  the two profiles are of different devices: /device:TPU:269 before, /device:TPU:29 now
where the time goes in v1:
time: 330 us
  waiting for transfers between devices  135 us (41%)
  blocking collectives  98.4 us (30%)
  starting transfers between devices  56.5 us (17%)
  between operations  14.5 us (4%)
  matrix products  12.1 us (4%)
  local copies, waits for them, and re-layouts  6.76 us (2%)
  other arithmetic  6.17 us (2%)
    ppermute x5, waiting for transfers between devices, gather_by_doubling(): other = lax.ppermute(cur, CTX, [(i, i ^ bit) for i in range(n)])  77.1 us
    all_to_all x1, blocking collectives, shards(): lax.all_to_all(outgoing, EXP, split_axis=0, concat_axis=0, tiled=True)  60.6 us
    all_to_all x1, waiting for transfers between devices, shards(): lax.all_to_all(share.reshape(n_exp, tok_dev, D), EXP, split_axis=0, conca...  43.8 us
    all_to_all x1, starting transfers between devices, shards(): lax.all_to_all(share.reshape(n_exp, tok_dev, D), EXP, split_axis=0, conca...  38.6 us
    all_to_all x1, blocking collectives, shards(): lax.all_to_all(jnp.stack([w_local] * lax.axis_size('zh')), 'zh', 0, 0)  37.8 us
    all_to_all x1, waiting for transfers between devices, shards(): lax.all_to_all(hidden.astype(jnp.bfloat16), EXP, split_axis=0, concat_axi...  14.6 us
    ppermute x5, starting transfers between devices, gather_by_doubling(): other = lax.ppermute(cur, CTX, [(i, i ^ bit) for i in range(n)])  11.8 us
  transfers between devices with their start and end apart: 8, of which 7 were waited for; matrix products, arithmetic and copies ran while one was open for 4% of the time, Pallas kernels for 0%

profile of v1, /device:TPU:29, one launch (start us, length us, event | category | flops | bytes accessed | tf_op | source)
XLA Modules:
  0.0 329.9 jit_solution(4438537352775024053)
XLA Ops:
  7.2 1.2 maximum_bitcast_fusion
  8.5 37.8 %all_to_all.20 = bf16[2,48,4096]{2,1,0:T(8,128)(2,1)} all-to-all(bf16[2,48,4096]{2,1,0:T(8,128)(2,1)S(1)} %pad_maximum_fusion), channel_id=1, replica_groups=mesh['zh'=2,'x'=4,'y'=4,'zl'=8,'c'=2] {'zh'}, dimensions={0} | all-to-all | bytes 1572864 | tf_op jit(solution)/shard_map/all_to_all | solution.py:74
  46.5 2.1 collective-permute-start
  48.5 17.2 %collective-permute-done = bf16[128,256]{1,0:T(8,128)(2,1)S(1)} collective-permute-done((bf16[128,256]{1,0:T(8,128)(2,1)S(1)}, bf16[128,256]{1,0:T(8,128)(2,1)S(1)}, u32[]{:S(2)}, u32[]{:S(2)}) %collective-permute-start) | collective-permute-done | bytes 65568 | tf_op jit(solution)/shard_map/ppermute | solution.py:42
  65.8 2.1 collective-permute-start.1
  67.9 5.5 %collective-permute-done.1 = bf16[256,256]{1,0:T(8,128)(2,1)S(1)} collective-permute-done((bf16[256,256]{1,0:T(8,128)(2,1)S(1)}, bf16[256,256]{1,0:T(8,128)(2,1)S(1)}, u32[]{:S(2)}, u32[]{:S(2)}) %collective-permute-start.1) | collective-permute-done | bytes 131104 | tf_op jit(solution)/shard_map/ppermute | solution.py:42
  73.5 2.8 collective-permute-start.2
  76.4 5.2 %collective-permute-done.2 = bf16[512,256]{1,0:T(8,128)(2,1)S(1)} collective-permute-done((bf16[512,256]{1,0:T(8,128)(2,1)S(1)}, bf16[512,256]{1,0:T(8,128)(2,1)S(1)}, u32[]{:S(2)}, u32[]{:S(2)}) %collective-permute-start.2) | collective-permute-done | bytes 262176 | tf_op jit(solution)/shard_map/ppermute | solution.py:42
  81.8 2.9 collective-permute-start.3
  84.9 21.5 %collective-permute-done.3 = bf16[1024,256]{1,0:T(8,128)(2,1)S(1)} collective-permute-done((bf16[1024,256]{1,0:T(8,128)(2,1)S(1)}, bf16[1024,256]{1,0:T(8,128)(2,1)S(1)}, u32[]{:S(2)}, u32[]{:S(2)}) %collective-permute-start.3) | collective-permute-done | bytes 524320 | tf_op jit(solution)/shard_map/ppermute | solution.py:42
  106.6 1.9 collective-permute-start.4
  108.9 0.8 broadcast_compare_fusion.1
  109.7 27.6 %collective-permute-done.4 = bf16[2048,256]{1,0:T(8,128)(2,1)S(1)} collective-permute-done((bf16[2048,256]{1,0:T(8,128)(2,1)S(1)}, bf16[2048,256]{1,0:T(8,128)(2,1)S(1)}, u32[]{:S(2)}, u32[]{:S(2)}) %collective-permute-start.4) | collective-permute-done | bytes 1048608 | tf_op jit(solution)/shard_map/ppermute | solution.py:42
  137.3 0.5 maximum_select_fusion
  139.3 0.4 fusion.14
  139.7 0.4 fusion.18
  140.2 0.4 fusion.12
  140.5 0.4 fusion.10
  141.7 1.5 fusion
  143.2 38.6 %all-to-all-start = ((bf16[16,8,4096]{2,1,0:T(8,128)(2,1)}), bf16[16,8,4096]{2,1,0:T(8,128)(2,1)S(1)}, u32[]{:S(2)}, u32[]{:S(2)}) async-start(bf16[16,8,4096]{2,1,0:T(8,128)(2,1)} %fusion), calls=%async_computation | async-start | bytes 2097152 | tf_op jit(solution)/shard_map/all_to_all | solution.py:131
  182.5 43.8 %all-to-all-done = bf16[16,8,4096]{2,1,0:T(8,128)(2,1)S(1)} async-done(((bf16[16,8,4096]{2,1,0:T(8,128)(2,1)}), bf16[16,8,4096]{2,1,0:T(8,128)(2,1)S(1)}, u32[]{:S(2)}, u32[]{:S(2)}) %all-to-all-start) | async-done | bytes 1048608 | tf_op jit(solution)/shard_map/all_to_all | solution.py:131
  226.6 1.3 convolution_convert_fusion.1
  227.9 1.4 reshape.364
  229.3 60.6 %all_to_all.21 = bf16[16,6,4096]{2,1,0:T(8,128)(2,1)} all-to-all(bf16[16,6,4096]{2,1,0:T(8,128)(2,1)S(1)} %reshape.364), channel_id=1, replica_groups=mesh['zh'=2,'x'=4,'y'=4,'zl'=8,'c'=2] {'zl','c'}, dimensions={0} | all-to-all | bytes 1572864 | tf_op jit(solution)/shard_map/all_to_all | solution.py:153
  289.9 1.4 reshape.387
  291.4 6.4 %fusion.22 = f32[96,16,2,2,24]{0,4,3,2,1:T(8,128)S(1)} fusion(bf16[16,2,2,24,4096]{4,3,2,1,0:T(8,128)(2,1)} %bitcast.297, bf16[96,4096,1,1,1]{1,0,2,3,4:T(8,128)(2,1)S(1)} %reshape.387), kind=kOutput, calls=%fused_computation.45 | convolution fusion | flops 1207959552 | bytes 13959168 | tf_op jit(solution)/shard_map/sd,fd->sf/dot_general | solution.py:155
  298.0 1.1 copy.54
  299.1 1.8 convert_element_type.76
  300.9 6.1 %all-to-all-start.3 = ((bf16[16,6,768]{2,1,0:T(8,128)(2,1)}), bf16[16,6,768]{2,1,0:T(8,128)(2,1)S(1)}, u32[]{:S(2)}, u32[]{:S(2)}) async-start(bf16[16,6,768]{2,1,0:T(8,128)(2,1)} %convert_element_type.76), calls=%async_computation.3 | async-start | bytes 393216 | tf_op jit(solution)/shard_map/all_to_all | solution.py:160
  307.0 14.6 %all-to-all-done.3 = bf16[16,6,768]{2,1,0:T(8,128)(2,1)S(1)} async-done(((bf16[16,6,768]{2,1,0:T(8,128)(2,1)}), bf16[16,6,768]{2,1,0:T(8,128)(2,1)S(1)}, u32[]{:S(2)}, u32[]{:S(2)}) %all-to-all-start.3) | async-done | bytes 147488 | tf_op jit(solution)/shard_map/all_to_all | solution.py:160
  321.6 0.7 gather_fusion
  322.3 0.7 fusion.43
  (64 shorter events, 4.6 us)
Async XLA Ops:
  7.2 134.5 %copy-start = (bf16[256,4096]{1,0:T(8,128)(2,1)S(1)}, bf16[256,4096]{1,0:T(8,128)(2,1)}, u32[]{:S(2)}) copy-start(bf16[256,4096]{1,0:T(8,128)(2,1)} %param.17) | copy-start | bytes 6291460
  7.2 284.2 %all-gather.2.cloned.1.call-start = ((), (), s32[]{:S(2)}) async-start(), calls=%async_computation.4 | async-start | bytes 13369344 | tf_op jit(solution)/shard_map/all_gather | solution.py:76
  7.2 39.2 %copy-start.5 = (bf16[128,256]{1,0:T(8,128)(2,1)S(1)}, bf16[128,256]{1,0:T(8,128)(2,1)}, u32[]{:S(2)}) copy-start(bf16[128,256]{1,0:T(8,128)(2,1)} %param.15) | copy-start | bytes 196612
  7.2 39.2 %copy-start.6 = (bf16[128,256]{1,0:T(8,128)(2,1)S(1)}, bf16[128,256]{1,0:T(8,128)(2,1)}, u32[]{:S(2)}) copy-start(bf16[128,256]{1,0:T(8,128)(2,1)} %param.14) | copy-start | bytes 196612
  8.5 76.2 %copy-start.8 = (s32[64]{0:T(128)S(1)}, s32[64]{0:T(128)}, u32[]{:S(2)}) copy-start(s32[64]{0:T(128)} %param.16) | copy-start | bytes 772
  8.5 76.3 %copy-start.9 = (s32[32]{0:T(128)S(1)}, s32[32]{0:T(128)}, u32[]{:S(2)}) copy-start(s32[32]{0:T(128)} %constant.180) | copy-start | bytes 388
  46.5 19.3 %collective-permute-start = (bf16[128,256]{1,0:T(8,128)(2,1)S(1)}, bf16[128,256]{1,0:T(8,128)(2,1)S(1)}, u32[]{:S(2)}, u32[]{:S(2)}) collective-permute-start(bf16[128,256]{1,0:T(8,128)(2,1)S(1)} %pad_maximum_fusion.1), channel_id=1, source_target_pairs={{0,256},{16,272},{32,288},{48,304},{64,320},{80,336},{96,352},{112... | collective-permute-start | bytes 196616 | tf_op jit(solution)/shard_map/ppermute | solution.py:42
  65.8 7.7 %collective-permute-start.1 = (bf16[256,256]{1,0:T(8,128)(2,1)S(1)}, bf16[256,256]{1,0:T(8,128)(2,1)S(1)}, u32[]{:S(2)}, u32[]{:S(2)}) collective-permute-start(bf16[256,256]{1,0:T(8,128)(2,1)S(1)} %maximum_select_fusion.4), channel_id=1, source_target_pairs={{0,128},{16,144},{32,160},{48,176},{64,192},{80,208},{96,224},{112... | collective-permute-start | bytes 393224 | tf_op jit(solution)/shard_map/ppermute | solution.py:42
  73.5 8.0 %collective-permute-start.2 = (bf16[512,256]{1,0:T(8,128)(2,1)S(1)}, bf16[512,256]{1,0:T(8,128)(2,1)S(1)}, u32[]{:S(2)}, u32[]{:S(2)}) collective-permute-start(bf16[512,256]{1,0:T(8,128)(2,1)S(1)} %maximum_select_fusion.3), channel_id=1, source_target_pairs={{0,64},{16,80},{32,96},{48,112},{64,0},{80,16},{96,32},{112,48},{1... | collective-permute-start | bytes 786440 | tf_op jit(solution)/shard_map/ppermute | solution.py:42
  81.8 24.6 %collective-permute-start.3 = (bf16[1024,256]{1,0:T(8,128)(2,1)S(1)}, bf16[1024,256]{1,0:T(8,128)(2,1)S(1)}, u32[]{:S(2)}, u32[]{:S(2)}) collective-permute-start(bf16[1024,256]{1,0:T(8,128)(2,1)S(1)} %maximum_select_fusion.2), channel_id=1, source_target_pairs={{0,32},{16,48},{32,0},{48,16},{64,96},{80,112},{96,64},{112,80},{1... | collective-permute-start | bytes 1572872 | tf_op jit(solution)/shard_map/ppermute | solution.py:42
  106.6 30.7 %collective-permute-start.4 = (bf16[2048,256]{1,0:T(8,128)(2,1)S(1)}, bf16[2048,256]{1,0:T(8,128)(2,1)S(1)}, u32[]{:S(2)}, u32[]{:S(2)}) collective-permute-start(bf16[2048,256]{1,0:T(8,128)(2,1)S(1)} %maximum_select_fusion.1), channel_id=1, source_target_pairs={{0,16},{16,0},{32,48},{48,32},{64,80},{80,64},{96,112},{112,96},{1... | collective-permute-start | bytes 3145736 | tf_op jit(solution)/shard_map/ppermute | solution.py:42
  109.7 28.2 %copy-start.10 = (bf16[128,256]{1,0:T(8,128)(2,1)S(1)}, bf16[128,256]{1,0:T(8,128)(2,1)}, u32[]{:S(2)}) copy-start(bf16[128,256]{1,0:T(8,128)(2,1)} %param.13) | copy-start | bytes 196612
  141.6 40.2 %copy-start.3 = (s32[8,8]{1,0:T(8,128)S(1)}, s32[8,8]{1,0:T(8,128)}, u32[]{:S(2)}) copy-start(s32[8,8]{1,0:T(8,128)} %param.21) | copy-start | bytes 772
  143.2 83.2 %copy-start.2 = (bf16[8,4096]{1,0:T(8,128)(2,1)S(1)}, bf16[8,4096]{1,0:T(8,128)(2,1)}, u32[]{:S(2)}) copy-start(bf16[8,4096]{1,0:T(8,128)(2,1)} %param.12) | copy-start | bytes 196612
  143.2 83.4 %copy-start.4 = (f32[4096]{0:T(1024)S(1)}, f32[4096]{0:T(1024)}, u32[]{:S(2)}) copy-start(f32[4096]{0:T(1024)} %param.18) | copy-start | bytes 49156
  143.2 83.1 %all-to-all-start = ((bf16[16,8,4096]{2,1,0:T(8,128)(2,1)}), bf16[16,8,4096]{2,1,0:T(8,128)(2,1)S(1)}, u32[]{:S(2)}, u32[]{:S(2)}) async-start(bf16[16,8,4096]{2,1,0:T(8,128)(2,1)} %fusion), calls=%async_computation | async-start | bytes 2097152 | tf_op jit(solution)/shard_map/all_to_all | solution.py:131
  226.6 63.4 %copy-start.1 = (bf16[8,4096]{1,0:T(8,128)(2,1)}, bf16[8,4096]{1,0:T(8,128)(2,1)S(1)}, u32[]{:S(2)}) copy-start(bf16[8,4096]{1,0:T(8,128)(2,1)S(1)} %get-tuple-element.9) | copy-start | bytes 196612
  298.0 24.4 %copy-start.7 = (f32[8,8]{1,0:T(8,128)S(1)}, f32[8,8]{1,0:T(8,128)}, u32[]{:S(2)}) copy-start(f32[8,8]{1,0:T(8,128)} %param.22) | copy-start | bytes 772
  300.9 20.7 %all-to-all-start.3 = ((bf16[16,6,768]{2,1,0:T(8,128)(2,1)}), bf16[16,6,768]{2,1,0:T(8,128)(2,1)S(1)}, u32[]{:S(2)}, u32[]{:S(2)}) async-start(bf16[16,6,768]{2,1,0:T(8,128)(2,1)} %convert_element_type.76), calls=%async_computation.3 | async-start | bytes 393216 | tf_op jit(solution)/shard_map/all_to_all | solution.py:160
Sparse Core Ops, SparseCore 0:
  46.5 138.1 all-gather.1
